TPU v7x, 128 devices: a whole 4x4x4 slice. The times are simulated.
128 devices in a mesh: dp: 16 (over z, y_lo, core), space: 8 (over x, y_hi).
Axes of the slice: x: 4, y: 4 (y_hi: 2, y_lo: 2; y = y_hi * 2 + y_lo), z: 4, core: 2. Of those that a mesh axis runs over, the one named last changes fastest.
Arguments:
- decoder_input: bfloat16 [16, 64, 16, 16, 128], P('dp', None, 'space'), may hold values from -6 to 6
- cotangent: bfloat16 [16, 64, 16, 16, 128], P('dp', None, 'space'), may hold values from -6 to 6
- encoder_input: bfloat16 [16, 64, 16, 16, 128], P('dp', None, 'space'), may hold values from -6 to 6
- decoder_weights: bfloat16 [2, 27, 4096], replicated, may hold values from -0.15625 to 0.15625
- other_grads: bfloat16 [16, 8, 12, 27, 4096], P('dp', 'space'), may hold values from -384 to 384
- assignment: int32 [12], replicated, may hold values from 0 to 31, as said below
- moment_first: float32 [32, 27, 4096], P('dp', None, 'space'), may hold values from -4 to 4
- moment_second: float32 [32, 27, 4096], P('dp', None, 'space'), may hold values from 0.02 to 2
- master_weights: float32 [32, 27, 4096], P('dp', None, 'space'), may hold values from -0.15625 to 0.15625
Outputs:
- input_grad: bfloat16 [16, 64, 16, 16, 128], P('dp', None, 'space')
- encoder_out: bfloat16 [16, 64, 16, 16, 128], P('dp', None, 'space')
- new_params: bfloat16 [12, 27, 4096], replicated
- new_first: float32 [32, 27, 4096], P('dp', None, 'space')
- new_second: float32 [32, 27, 4096], P('dp', None, 'space')
- new_master: float32 [32, 27, 4096], P('dp', None, 'space')
Inputs may be any that keep to these rules, and one draw needn't show every extreme that they name: `assignment`: the values are distinct; value j places the tensor with owner j // 2 in that owner's slot j % 2; some owner holds 2 tensors.
All inputs are finite; a program needn't handle non-finite values.
Results may differ from a plain program's by a relative error of at most 0.005.
Values may be sent and summed in bfloat16 or wider, within the bound.
No kernel may reach another device: no remote copies, remote signals or barrier semaphores. Data moves between devices by JAX's collectives and lax.ppermute only.
A program may use at most 128 MiB of HBM per device.

v0:
```python
import math
import jax
import jax.numpy as jnp
from jax import lax
from jax.sharding import PartitionSpec as P

learn_rate = 0.002
decay_rate = 0.1
epsilon = 1e-08
bias_one = 1.0 - (0.9**50) ** 2
bias_two = 1.0 - (0.999**50) ** 2
volume_dims = ("NCDHW", "OIDHW", "NCDHW")
swapped_dims = ("CNDHW", "OIDHW", "NCDHW")


def padded_2(block, sides, width):
    for axis, dim in sides:
        count = lax.axis_size(axis)
        forward = [(i, i + 1) for i in range(count - 1)]
        forward.append((count - 1, 0))
        backward = [(target, source) for source, target in forward]
        low = lax.ppermute(
            lax.slice_in_dim(block, block.shape[dim] - width, None, axis=dim), axis, forward
        )
        high = lax.ppermute(lax.slice_in_dim(block, 0, width, axis=dim), axis, backward)
        block = jnp.concatenate([low, block, high], axis=dim)
    return block


def widened(field):
    rimmed = padded_2(field, (("space", 1),), 1)
    return jnp.pad(rimmed, ((0, 0), (0, 0), (1, 1), (1, 1)), mode="wrap")


def forward_local(padded, kernel):
    channels = kernel.shape[1]
    weights = kernel.reshape(3, 3, 3, channels, channels).transpose(3, 4, 0, 1, 2)
    result = lax.conv_general_dilated(
        padded[None],
        weights,
        (1, 1, 1),
        "VALID",
        dimension_numbers=volume_dims,
        preferred_element_type=jnp.float32,
    )
    return result[0].reshape(channels, -1)


def backward_local(padded, kernel):
    channels = kernel.shape[1]
    weights = kernel.reshape(3, 3, 3, channels, channels)[::-1, ::-1, ::-1].transpose(4, 3, 0, 1, 2)
    result = lax.conv_general_dilated(
        padded[None],
        weights,
        (1, 1, 1),
        "VALID",
        dimension_numbers=volume_dims,
        preferred_element_type=jnp.float32,
    )
    return result[0].reshape(channels, -1)


def kernel_grad(grad_field, padded):
    channels = grad_field.shape[0]
    result = lax.conv_general_dilated(
        padded[None],
        grad_field[:, None],
        (1, 1, 1),
        "VALID",
        dimension_numbers=swapped_dims,
        preferred_element_type=jnp.float32,
    )
    return result.transpose(2, 3, 4, 1, 0).reshape(27, channels, channels)


def space_scatter(block):
    count = lax.axis_size("space")
    lead = block.shape[:-1]
    split = block.reshape(lead + (count, block.shape[-1] // count))
    split = jnp.moveaxis(split, -2, 0)
    return lax.psum_scatter(split, "space", scatter_dimension=0, tiled=True)[0]


def space_gather(block):
    count = lax.axis_size("space")
    lead = block.shape[:-1]
    whole = lax.all_gather(block, "space", axis=0, tiled=False)
    whole = jnp.moveaxis(whole, 0, -2)
    return whole.reshape(lead + (count * block.shape[-1],))


def adamw(grads, first, second, master):
    new_first = 0.9 * first + 0.1 * grads
    new_second = 0.999 * second + 0.001 * grads * grads
    update = new_first / bias_one / (jnp.sqrt(new_second / bias_two) + epsilon)
    new_master = master - learn_rate * (update + decay_rate * master)
    return (new_first, new_second, new_master)


def owner_rows(grads, assign, owner, first, second, master):
    slot_count = first.shape[0]
    local = assign % slot_count
    pick = lambda state: jnp.take(state, local, axis=0)
    rows = adamw(grads, pick(first), pick(second), pick(master))[2].astype(jnp.bfloat16)
    mine = (assign // slot_count == owner)[:, None, None]
    return jnp.where(mine, rows, jnp.zeros_like(rows))


def per_device(
    decoder_input,
    cotangent,
    encoder_input,
    decoder_weights,
    other_grads,
    assignment,
    moment_first,
    moment_second,
    master_weights,
):
    field_shape = decoder_input.shape[1:]
    channels = field_shape[0]
    thick = field_shape[1]
    kernel_a = decoder_weights[0].reshape(27, channels, channels)
    kernel_b = decoder_weights[1].reshape(27, channels, channels)
    dec_field = decoder_input[0]
    dec_wide = widened(dec_field)
    preact = forward_local(dec_wide, kernel_a)
    sigma = jax.nn.sigmoid(preact)
    hidden = (preact * sigma).astype(jnp.bfloat16).reshape(field_shape)
    cot_field = cotangent[0]
    grad_b = kernel_grad(cot_field, widened(hidden))
    grad_hidden = backward_local(widened(cot_field), kernel_b)
    grad_pre = (
        (grad_hidden * sigma * (1.0 + preact * (1.0 - sigma)))
        .astype(jnp.bfloat16)
        .reshape(field_shape)
    )
    grad_a = kernel_grad(grad_pre, dec_wide)
    input_grad = backward_local(widened(grad_pre), kernel_a)
    input_grad = input_grad.astype(jnp.bfloat16).reshape((1,) + field_shape)
    replicas = lax.axis_size("dp")
    slabs = lax.axis_size("space")
    scale = 1.0 / math.sqrt(replicas * thick * slabs * field_shape[2] * field_shape[3])
    owner = lax.axis_index("dp")
    other_tot = lax.psum(space_scatter(other_grads[0, 0]), "dp").astype(jnp.float32)
    enc_rows = owner_rows(
        other_tot[2:4] * scale, assignment[2:4], owner, moment_first, moment_second, master_weights
    )
    enc_params = space_gather(lax.psum(enc_rows, "dp"))
    kernel_c = enc_params[0].reshape(27, channels, channels)
    kernel_d = enc_params[1].reshape(27, channels, channels)
    ab_grads = jnp.stack([grad_a.reshape(27, -1), grad_b.reshape(27, -1)]).astype(jnp.bfloat16)
    ab_tot = lax.psum(space_scatter(ab_grads), "dp").astype(jnp.float32)
    totals = jnp.concatenate([other_tot[:2] + ab_tot, other_tot[2:]]) * scale
    slot_count = moment_first.shape[0]
    slot_ids = owner * slot_count + jnp.arange(slot_count)
    match = assignment[None, :] == slot_ids[:, None]
    owned = jnp.sum(jnp.where(match[:, :, None, None], totals[None], 0.0), axis=1)
    new_first, new_second, new_master = adamw(owned, moment_first, moment_second, master_weights)
    late = jnp.array([0, 1] + list(range(4, assignment.shape[0])))
    late_assign = assignment[late]
    late_local = jnp.take(new_master.astype(jnp.bfloat16), late_assign % slot_count, axis=0)
    late_rows = jnp.where(
        (late_assign // slot_count == owner)[:, None, None], late_local, jnp.zeros_like(late_local)
    )
    late_params = space_gather(lax.psum(late_rows, "dp"))
    new_params = jnp.concatenate([late_params[:2], enc_params, late_params[2:]])
    enc_field = encoder_input[0]
    first = forward_local(widened(enc_field), kernel_c)
    activ = (first * jax.nn.sigmoid(first)).astype(jnp.bfloat16).reshape(field_shape)
    second = forward_local(widened(activ), kernel_d)
    encoder_out = (enc_field.reshape(channels, -1).astype(jnp.float32) + second).astype(
        jnp.bfloat16
    )
    encoder_out = encoder_out.reshape((1,) + field_shape)
    return (input_grad, encoder_out, new_params, new_first, new_second, new_master)


def solution(mesh):
    in_specs = (
        P("dp", None, "space", None, None),
        P("dp", None, "space", None, None),
        P("dp", None, "space", None, None),
        P(),
        P("dp", "space", None, None, None),
        P(),
        P("dp", None, "space"),
        P("dp", None, "space"),
        P("dp", None, "space"),
    )
    out_specs = (
        P("dp", None, "space", None, None),
        P("dp", None, "space", None, None),
        P(),
        P("dp", None, "space"),
        P("dp", None, "space"),
        P("dp", None, "space"),
    )
    return jax.shard_map(
        per_device, mesh=mesh, in_specs=in_specs, out_specs=out_specs, check_vma=False
    )
```

profile of v0, /device:TPU:0, one launch (start us, length us, event | category | flops | bytes accessed | tf_op | source)
XLA Modules:
  0.0 786.5 jit_solution(13005885202175331573)
XLA Ops:
  9.1 3.3 collective-permute-start
  12.4 2.3 collective-permute-start.1
  18.0 4.4 collective-permute-start.3
  22.4 4.7 reshape_squeeze.21
  27.2 4.5 copy.311
  43.2 2.5 copy.209
  51.8 5.6 collective-permute-start.7
  59.4 5.7 maximum_bitcast_fusion
  65.1 7.8 copy.231
  75.2 4.6 fusion.53
  85.1 4.6 fusion.140
  89.7 5.9 copy.232
  95.6 2.9 pad.2.clone
  99.5 8.6 %fusion.50 = f32[2,16,8,17,64]{4,2,3,1,0:T(8,128)S(1)} fusion(bf16[3,3,3,64,64]{4,3,2,1,0:T(8,128)(2,1)S(1)} %copy-done.33, bf16[64,4,18,1,7,2]{0,4,5,2,1,3:T(8,128)(2,1)S(1)} %slice.228, bf16[64,4,18,1,8,17]{0,4,5,2,1,3:T(8,128)(2,1)S(1)} %copy.170, pred[8,17]{0,1:T(8,128)(4,1)S(1)} %copy-done.44), kind=kOutput, calls=%fused_computation.57 | convolution fusion | flops 967073792 | bytes 2717832 | tf_op jit(solution)/shard_map/conv_general_dilated | solution.py:38
  110.0 3.7 copy.229
  113.8 3.0 fusion.76
  116.8 5.2 fusion.139
  122.4 2.6 copy.203
  125.0 9.1 %copy.202 = bf16[1,64,4,18,130]{1,0,4,3,2:T(2,128)(2,1)} copy(bf16[1,64,4,18,130]{4,1,3,2,0:T(8,128)(2,1)S(1)} %copy-done.12) | data formatting | bytes 2396160 | tf_op jit(solution)/shard_map/broadcast_in_dim | solution.py:39
  135.0 5.6 collective-permute-start.11
  142.7 2.2 pad_maximum_fusion.3
  144.9 2.4 fusion.114
  148.4 30.6 %convolution_convert_fusion.1 = bf16[3,3,3,64,64]{3,4,2,1,0:T(8,128)(2,1)} fusion(bf16[1,64,4,18,130]{1,0,4,3,2:T(2,128)(2,1)S(1)} %copy-done.15, bf16[64,1,2,16,128]{0,1,4,3,2:T(2,128)(2,1)S(1)} %copy-done.24), kind=kOutput, calls=%fused_computation.66 | convolution fusion | flops 906080256 | bytes 1943552 | tf_op jit(solution)/shard_map/transpose | solution.py:73
  179.0 5.2 maximum_bitcast_fusion.1
  188.2 5.7 copy.233
  193.9 2.9 pad.6.clone
  198.9 5.6 collective-permute-start.5
  208.7 9.4 %copy.208 = bf16[1,64,4,18,130]{1,0,4,3,2:T(2,128)(2,1)} copy(bf16[1,64,4,18,130]{4,1,3,2,0:T(8,128)(2,1)S(1)} %maximum_bitcast_fusion.4) | data formatting | bytes 2396160 | tf_op jit(solution)/shard_map/broadcast_in_dim | solution.py:66
  218.0 32.9 %convolution_convert_fusion = bf16[3,3,3,64,64]{3,4,2,1,0:T(8,128)(2,1)S(1)} fusion(bf16[1,64,4,18,130]{1,0,4,3,2:T(2,128)(2,1)} %copy.208, bf16[64,1,2,16,128]{0,1,4,3,2:T(2,128)(2,1)} %copy.209), kind=kOutput, calls=%fused_computation.65 | convolution fusion | flops 906080256 | bytes 1943552 | tf_op jit(solution)/shard_map/transpose | solution.py:73
  256.0 2.7 maximum_bitcast_fusion.2
  258.7 4.5 copy.234
  265.7 72.5 %all-reduce.11.cloned.1.call-done = bf16[8,2,27,512]{3,1,2,0:T(2,128)(2,1)} async-done(((bf16[8,2,27,512]{3,1,2,0:T(2,128)(2,1)}), bf16[8,2,27,512]{3,1,2,0:T(2,128)(2,1)}) %all-reduce.11.cloned.1.call-update) | async-done | bytes 442384
  340.4 116.6 %all-reduce.7.cloned.1.call-done = bf16[12,27,512]{2,1,0:T(8,128)(2,1)} async-done(((bf16[12,27,512]{2,1,0:T(8,128)(2,1)}), bf16[12,27,512]{2,1,0:T(8,128)(2,1)}) %all-reduce.7.cloned.1.call-update) | async-done | bytes 331792 | tf_op jit(solution)/shard_map/psum | solution.py:145
  460.0 5.4 select_convert_fusion
  466.6 112.2 %all-reduce.13.cloned.1.call-done = (bf16[1,2,27,512]{3,2,1,0:T(8,128)(2,1)}, bf16[2,27,512]{2,1,0:T(8,128)(2,1)}) async-done(((bf16[1,2,27,512]{3,2,1,0:T(8,128)(2,1)}, bf16[2,27,512]{2,1,0:T(8,128)(2,1)}), (bf16[1,2,27,512]{3,2,1,0:T(8,128)(2,1)}, bf16[2,27,512]{2,1,0:T(8,128)(2,1)})) %all-reduce.13.cloned.1.call-update) | async-done | bytes 110608 | tf_op jit(solution)/shard_map/psum | solution.py:149
  582.4 34.9 %all_gather.13 = bf16[8,2,27,512]{3,1,2,0:T(2,128)(2,1)S(1)} all-gather(bf16[1,2,27,512]{3,1,2,0:T(2,128)(2,1)S(1)} %copy.188), channel_id=1, replica_groups=mesh['dp'=16,'space'=8] {'space'}, dimensions={0}, use_global_device_ids=true | all-gather | bytes 497664 | tf_op jit(solution)/shard_map/all_gather | solution.py:87
  618.2 79.7 %all-reduce.9.cloned.1.call-done = bf16[1,10,27,512]{3,2,1,0:T(8,128)(2,1)} async-done(((bf16[1,10,27,512]{3,2,1,0:T(8,128)(2,1)}), bf16[1,10,27,512]{3,2,1,0:T(8,128)(2,1)}) %all-reduce.9.cloned.1.call-update) | async-done | bytes 276496 | tf_op jit(solution)/shard_map/psum | solution.py:166
  697.9 10.3 %fusion.47 = f32[2,16,8,17,64]{4,2,3,1,0:T(8,128)S(1)} fusion(bf16[3,3,3,64,64]{4,3,2,1,0:T(8,128)(2,1)S(1)} %reshape_reshape_squeeze.15, bf16[64,4,18,1,7,2]{0,4,5,2,1,3:T(8,128)(2,1)S(1)} %copy-done.35, bf16[64,4,18,1,8,17]{0,4,5,2,1,3:T(8,128)(2,1)} %copy-done.22, pred[8,17]{0,1:T(8,128)(4,1)S(1)} %copy-done.45), kind=kOutput, calls=%fused_computation.56 | convolution fusion | flops 967073792 | bytes 2717832 | tf_op jit(solution)/shard_map/conv_general_dilated | solution.py:38
  713.4 2.8 collective-permute-start.8
  716.2 2.8 collective-permute-start.9
  720.2 3.3 copy.222
  727.9 3.1 collective-permute-done.9
  733.7 2.7 maximum_bitcast_fusion.3
  736.5 4.8 copy.235
  742.9 8.6 %fusion.42 = f32[2,16,8,17,64]{4,2,3,1,0:T(8,128)S(1)} fusion(bf16[3,3,3,64,64]{4,3,2,1,0:T(8,128)(2,1)S(1)} %reshape_reshape_squeeze.16, bf16[64,4,18,1,7,2]{0,4,5,2,1,3:T(8,128)(2,1)S(1)} %slice.252, bf16[64,4,18,1,8,17]{0,4,5,2,1,3:T(8,128)(2,1)S(1)} %copy.197, pred[8,17]{0,1:T(8,128)(4,1)S(1)} %copy-done.45), kind=kOutput, calls=%fused_computation.55 | convolution fusion | flops 967073792 | bytes 2717832 | tf_op jit(solution)/shard_map/conv_general_dilated | solution.py:38
  755.0 10.5 %all-gather.2.cloned.1.call-done = bf16[8,10,27,512]{3,2,1,0:T(8,128)(2,1)} async-done(((bf16[1,10,27,512]{3,2,1,0:T(8,128)(2,1)}), bf16[8,10,27,512]{3,2,1,0:T(8,128)(2,1)}) %all-gather.2.cloned.1.call-update) | async-done | bytes 2211856 | tf_op jit(solution)/shard_map/all_gather | solution.py:87
  773.0 3.0 pad_maximum_fusion
  776.0 3.2 copy.224
  (232 shorter events, 93.5 us)
Async XLA Ops:
  7.2 247.8 %reduce-scatter.2.cloned.1.call-start = ((), (), s32[]{:S(2)}) async-start(), calls=%async_computation.1 | async-start | bytes 3538944 | tf_op jit(solution)/shard_map/reduce_scatter | solution.py:81
  9.1 42.8 %collective-permute-start = (bf16[64,1,16,128]{3,2,1,0:T(8,128)(2,1)}, bf16[64,1,16,128]{3,2,1,0:T(8,128)(2,1)S(1)}, u32[]{:S(2)}, u32[]{:S(2)}) collective-permute-start(bf16[64,1,16,128]{3,2,1,0:T(8,128)(2,1)} %get-tuple-element.78), channel_id=1, source_target_pairs={{0,1},{1,2},{2,3},{3,4},{4,5},{5,6},{6,7},{7,0},{8,9},{9,10},{10,1... | collective-permute-start | bytes 786440 | tf_op jit(solution)/shard_map/ppermute | solution.py:22
  12.4 45.1 %collective-permute-start.1 = (bf16[64,1,16,128]{3,2,1,0:T(8,128)(2,1)}, bf16[64,1,16,128]{3,2,1,0:T(8,128)(2,1)S(1)}, u32[]{:S(2)}, u32[]{:S(2)}) collective-permute-start(bf16[64,1,16,128]{3,2,1,0:T(8,128)(2,1)} %get-tuple-element.79), channel_id=1, source_target_pairs={{1,0},{2,1},{3,2},{4,3},{5,4},{6,5},{7,6},{0,7},{9,8},{10,9},{11,1... | collective-permute-start | bytes 786440 | tf_op jit(solution)/shard_map/ppermute | solution.py:25
  16.8 65.7 %collective-permute-start.2 = (bf16[64,1,16,128]{3,0,2,1:T(8,128)(2,1)}, bf16[64,1,16,128]{3,0,2,1:T(8,128)(2,1)}, u32[]{:S(2)}, u32[]{:S(2)}) collective-permute-start(bf16[64,1,16,128]{3,0,2,1:T(8,128)(2,1)} %get-tuple-element.76), channel_id=1, source_target_pairs={{0,1},{1,2},{2,3},{3,4},{4,5},{5,6},{6,7},{7,0},{8,9},{9,10},{10,1... | collective-permute-start | bytes 786440 | tf_op jit(solution)/shard_map/ppermute | solution.py:22
  18.0 64.5 %collective-permute-start.3 = (bf16[64,1,16,128]{3,0,2,1:T(8,128)(2,1)}, bf16[64,1,16,128]{3,0,2,1:T(8,128)(2,1)}, u32[]{:S(2)}, u32[]{:S(2)}) collective-permute-start(bf16[64,1,16,128]{3,0,2,1:T(8,128)(2,1)} %get-tuple-element.77), channel_id=1, source_target_pairs={{1,0},{2,1},{3,2},{4,3},{5,4},{6,5},{7,6},{0,7},{9,8},{10,9},{11,1... | collective-permute-start | bytes 786440 | tf_op jit(solution)/shard_map/ppermute | solution.py:25
  31.7 306.6 %all-reduce.11.cloned.1.call-start = ((), (), s32[]{:S(2)}) async-start(), calls=%async_computation.5 | async-start | bytes 884736
  33.5 9.6 %copy-start.1 = (bf16[1,64,2,16,128]{4,3,2,1,0:T(8,128)(2,1)S(1)}, bf16[1,64,2,16,128]{4,3,2,1,0:T(8,128)(2,1)}, u32[]{:S(2)}) copy-start(bf16[1,64,2,16,128]{4,3,2,1,0:T(8,128)(2,1)} %param.13) | copy-start | bytes 1572868
  33.5 107.1 %collective-permute-start.6 = (bf16[64,1,16,128]{3,2,1,0:T(8,128)(2,1)}, bf16[64,1,16,128]{3,2,1,0:T(8,128)(2,1)}, u32[]{:S(2)}, u32[]{:S(2)}) collective-permute-start(bf16[64,1,16,128]{3,2,1,0:T(8,128)(2,1)} %get-tuple-element.70), channel_id=1, source_target_pairs={{0,1},{1,2},{2,3},{3,4},{4,5},{5,6},{6,7},{7,0},{8,9},{9,10},{10,1... | collective-permute-start | bytes 786440 | tf_op jit(solution)/shard_map/ppermute | solution.py:22
  38.5 7.2 copy-start.8
  40.7 6.7 copy-start.6
  43.2 5.8 copy-start.4
  43.2 7.4 copy-start.43
  51.8 88.8 %collective-permute-start.7 = (bf16[64,1,16,128]{3,2,1,0:T(8,128)(2,1)}, bf16[64,1,16,128]{3,2,1,0:T(8,128)(2,1)}, u32[]{:S(2)}, u32[]{:S(2)}) collective-permute-start(bf16[64,1,16,128]{3,2,1,0:T(8,128)(2,1)} %get-tuple-element.71), channel_id=1, source_target_pairs={{1,0},{2,1},{3,2},{4,3},{5,4},{6,5},{7,6},{0,7},{9,8},{10,9},{11,1... | collective-permute-start | bytes 786440 | tf_op jit(solution)/shard_map/ppermute | solution.py:25
  116.8 5.2 copy-start.10
  116.8 5.2 copy-start.11
  125.0 9.1 %copy-start.18 = (bf16[64,2,16,128]{3,2,1,0:T(8,128)(2,1)S(1)}, bf16[64,2,16,128]{3,2,1,0:T(8,128)(2,1)}, u32[]{:S(2)}) copy-start(bf16[64,2,16,128]{3,2,1,0:T(8,128)(2,1)} %get-tuple-element.60) | copy-start | bytes 1572868
  135.0 69.5 %collective-permute-start.10 = (bf16[64,1,16,128]{3,2,1,0:T(8,128)(2,1)}, bf16[64,1,16,128]{3,2,1,0:T(8,128)(2,1)}, u32[]{:S(2)}, u32[]{:S(2)}) collective-permute-start(bf16[64,1,16,128]{3,2,1,0:T(8,128)(2,1)} %get-tuple-element.72), channel_id=1, source_target_pairs={{0,1},{1,2},{2,3},{3,4},{4,5},{5,6},{6,7},{7,0},{8,9},{9,10},{10,1... | collective-permute-start | bytes 786440 | tf_op jit(solution)/shard_map/ppermute | solution.py:22
  135.0 69.5 %collective-permute-start.11 = (bf16[64,1,16,128]{3,2,1,0:T(8,128)(2,1)}, bf16[64,1,16,128]{3,2,1,0:T(8,128)(2,1)}, u32[]{:S(2)}, u32[]{:S(2)}) collective-permute-start(bf16[64,1,16,128]{3,2,1,0:T(8,128)(2,1)} %get-tuple-element.73), channel_id=1, source_target_pairs={{1,0},{2,1},{3,2},{4,3},{5,4},{6,5},{7,6},{0,7},{9,8},{10,9},{11,1... | collective-permute-start | bytes 786440 | tf_op jit(solution)/shard_map/ppermute | solution.py:25
  142.7 4.6 copy-start.24
  148.4 30.6 %copy-start.3 = (bf16[1,64,2,16,128]{4,3,2,1,0:T(8,128)(2,1)S(1)}, bf16[1,64,2,16,128]{4,3,2,1,0:T(8,128)(2,1)}, u32[]{:S(2)}) copy-start(bf16[1,64,2,16,128]{4,3,2,1,0:T(8,128)(2,1)} %param.14) | copy-start | bytes 1572868
  148.4 30.6 %copy-start.13 = (bf16[64,4,18,1]{3,2,1,0:T(8,128)(2,1)S(1)}, bf16[64,4,18,1]{3,2,1,0:T(8,128)(2,1)}, u32[]{:S(2)}) copy-start(bf16[64,4,18,1]{3,2,1,0:T(8,128)(2,1)} %get-tuple-element.42) | copy-start | bytes 27652
  148.4 30.6 %copy-start.14 = (bf16[64,4,18,1]{3,2,1,0:T(8,128)(2,1)S(1)}, bf16[64,4,18,1]{3,2,1,0:T(8,128)(2,1)}, u32[]{:S(2)}) copy-start(bf16[64,4,18,1]{3,2,1,0:T(8,128)(2,1)} %get-tuple-element.43) | copy-start | bytes 27652
  148.4 30.6 %copy-start.27 = (bf16[64,4,1,128]{3,2,1,0:T(2,128)(2,1)S(1)}, bf16[64,4,1,128]{3,2,1,0:T(2,128)(2,1)}, u32[]{:S(2)}) copy-start(bf16[64,4,1,128]{3,2,1,0:T(2,128)(2,1)} %copy-done.26) | copy-start | bytes 196612
  148.4 30.6 %copy-start.29 = (bf16[64,4,1,128]{3,2,1,0:T(2,128)(2,1)S(1)}, bf16[64,4,1,128]{3,2,1,0:T(2,128)(2,1)}, u32[]{:S(2)}) copy-start(bf16[64,4,1,128]{3,2,1,0:T(2,128)(2,1)} %copy-done.28) | copy-start | bytes 196612
  196.8 7.7 copy-start.19
  197.2 8.8 %copy-start.22 = (bf16[64,4,18,1,8,17]{0,4,5,2,1,3:T(8,128)(2,1)}, bf16[64,4,18,1,8,17]{0,4,5,2,1,3:T(8,128)(2,1)S(1)}, u32[]{:S(2)}) copy-start(bf16[64,4,18,1,8,17]{0,4,5,2,1,3:T(8,128)(2,1)S(1)} %copy.183) | copy-start | bytes 3760132
  198.9 53.8 %collective-permute-start.4 = (bf16[64,1,16,128]{3,2,1,0:T(8,128)(2,1)}, bf16[64,1,16,128]{3,2,1,0:T(8,128)(2,1)}, u32[]{:S(2)}, u32[]{:S(2)}) collective-permute-start(bf16[64,1,16,128]{3,2,1,0:T(8,128)(2,1)} %get-tuple-element.74), channel_id=1, source_target_pairs={{0,1},{1,2},{2,3},{3,4},{4,5},{5,6},{6,7},{7,0},{8,9},{9,10},{10,1... | collective-permute-start | bytes 786440 | tf_op jit(solution)/shard_map/ppermute | solution.py:22
  198.9 53.8 %collective-permute-start.5 = (bf16[64,1,16,128]{3,2,1,0:T(8,128)(2,1)}, bf16[64,1,16,128]{3,2,1,0:T(8,128)(2,1)}, u32[]{:S(2)}, u32[]{:S(2)}) collective-permute-start(bf16[64,1,16,128]{3,2,1,0:T(8,128)(2,1)} %get-tuple-element.75), channel_id=1, source_target_pairs={{1,0},{2,1},{3,2},{4,3},{5,4},{6,5},{7,6},{0,7},{9,8},{10,9},{11,1... | collective-permute-start | bytes 786440 | tf_op jit(solution)/shard_map/ppermute | solution.py:25
  218.0 33.5 %copy-start.30 = (bf16[1,27,8,512]{3,2,1,0:T(8,128)(2,1)S(1)}, bf16[1,27,8,512]{3,2,1,0:T(8,128)(2,1)}, u32[]{:S(2)}) copy-start(bf16[1,27,8,512]{3,2,1,0:T(8,128)(2,1)} %stack.7) | copy-start | bytes 663556
  254.1 202.9 %all-reduce.7.cloned.1.call-start = ((), (), s32[]{:S(2)}) async-start(), calls=%async_computation.2 | async-start | bytes 786432 | tf_op jit(solution)/shard_map/psum | solution.py:145
  255.0 323.9 %all-reduce.13.cloned.1.call-start = ((), (), s32[]{:S(2)}) async-start(), calls=%async_computation.6 | async-start | bytes 262144 | tf_op jit(solution)/shard_map/psum | solution.py:149
  264.5 193.5 %copy-start.31 = (f32[2,27,512]{2,0,1:T(2,128)S(1)}, f32[2,27,512]{2,0,1:T(2,128)}, u32[]{:S(2)}) copy-start(f32[2,27,512]{2,0,1:T(2,128)} %gather_fusion.2) | copy-start | bytes 331780
  264.6 193.5 %copy-start.32 = (f32[2,27,512]{2,0,1:T(2,128)S(1)}, f32[2,27,512]{2,0,1:T(2,128)}, u32[]{:S(2)}) copy-start(f32[2,27,512]{2,0,1:T(2,128)} %gather_fusion.3) | copy-start | bytes 331780
  264.6 193.5 %copy-start.40 = (pred[2]{0:T(512)(128)(4,1)S(1)}, pred[2]{0:T(512)(128)(4,1)}, u32[]{:S(2)}) copy-start(pred[2]{0:T(512)(128)(4,1)} %get-tuple-element.39) | copy-start | bytes 10
  264.6 193.5 %copy-start.41 = (pred[2]{0:T(512)(128)(4,1)S(1)}, pred[2]{0:T(512)(128)(4,1)}, u32[]{:S(2)}) copy-start(pred[2]{0:T(512)(128)(4,1)} %fusion.99) | copy-start | bytes 10
  264.9 195.0 %copy-start.45 = (pred[8,17]{0,1:T(8,128)(4,1)S(1)}, pred[8,17]{0,1:T(8,128)(4,1)}, u32[]{:S(2)}) copy-start(pred[8,17]{0,1:T(8,128)(4,1)} %constant.141) | copy-start | bytes 412
  459.9 238.0 %all-reduce.9.cloned.1.call-start = ((), (), s32[]{:S(2)}) async-start(), calls=%async_computation.3 | async-start | bytes 655360 | tf_op jit(solution)/shard_map/psum | solution.py:166
  465.4 114.4 %copy-start.37 = (pred[2,12]{0,1:T(8,128)(4,1)S(1)}, pred[2,12]{0,1:T(8,128)(4,1)}, u32[]{:S(2)}) copy-start(pred[2,12]{0,1:T(8,128)(4,1)} %broadcast_compare_fusion) | copy-start | bytes 76
  466.5 113.9 %copy-start.5 = (f32[2,27,512]{2,0,1:T(2,128)S(1)}, f32[2,27,512]{2,0,1:T(2,128)}, u32[]{:S(2)}) copy-start(f32[2,27,512]{2,0,1:T(2,128)} %param.19) | copy-start | bytes 331780
  466.5 113.9 %copy-start.7 = (f32[2,27,512]{2,0,1:T(2,128)S(1)}, f32[2,27,512]{2,0,1:T(2,128)}, u32[]{:S(2)}) copy-start(f32[2,27,512]{2,0,1:T(2,128)} %param.18) | copy-start | bytes 331780
  466.5 114.0 %copy-start.9 = (f32[2,27,512]{2,0,1:T(2,128)S(1)}, f32[2,27,512]{2,0,1:T(2,128)}, u32[]{:S(2)}) copy-start(f32[2,27,512]{2,0,1:T(2,128)} %param.20) | copy-start | bytes 331780
  466.6 114.7 %copy-start.38 = (pred[10]{0:T(512)(128)(4,1)S(1)}, pred[10]{0:T(512)(128)(4,1)}, u32[]{:S(2)}) copy-start(pred[10]{0:T(512)(128)(4,1)} %get-tuple-element.82) | copy-start | bytes 34
  466.6 114.7 %copy-start.39 = (pred[10]{0:T(512)(128)(4,1)S(1)}, pred[10]{0:T(512)(128)(4,1)}, u32[]{:S(2)}) copy-start(pred[10]{0:T(512)(128)(4,1)} %get-tuple-element.83) | copy-start | bytes 34
  581.4 116.6 %copy-start.35 = (bf16[64,4,18,1,7,2]{0,4,5,2,1,3:T(8,128)(2,1)S(1)}, bf16[64,4,18,1,7,2]{0,4,5,2,1,3:T(8,128)(2,1)}, u32[]{:S(2)}) copy-start(bf16[64,4,18,1,7,2]{0,4,5,2,1,3:T(8,128)(2,1)} %slice.242) | copy-start | bytes 387076
  582.2 183.3 %all-gather.2.cloned.1.call-start = ((), (), s32[]{:S(2)}) async-start(), calls=%async_computation.4 | async-start | bytes 2949120 | tf_op jit(solution)/shard_map/all_gather | solution.py:87
  711.1 8.0 %copy-start.20 = (bf16[2,16,8,17,64]{4,1,3,2,0:T(8,128)(2,1)S(1)}, bf16[2,16,8,17,64]{4,1,3,2,0:T(8,128)(2,1)}, u32[]{:S(2)}) copy-start(bf16[2,16,8,17,64]{4,1,3,2,0:T(8,128)(2,1)} %copy.179) | copy-start | bytes 1671172
  713.4 14.5 %collective-permute-start.8 = (bf16[64,1,16,128]{3,2,1,0:T(8,128)(2,1)}, bf16[64,1,16,128]{3,2,1,0:T(8,128)(2,1)}, u32[]{:S(2)}, u32[]{:S(2)}) collective-permute-start(bf16[64,1,16,128]{3,2,1,0:T(8,128)(2,1)} %get-tuple-element.68), channel_id=1, source_target_pairs={{0,1},{1,2},{2,3},{3,4},{4,5},{5,6},{6,7},{7,0},{8,9},{9,10},{10,1... | collective-permute-start | bytes 786440 | tf_op jit(solution)/shard_map/ppermute | solution.py:22
  716.2 14.8 %collective-permute-start.9 = (bf16[64,1,16,128]{3,2,1,0:T(8,128)(2,1)S(1)}, bf16[64,1,16,128]{3,2,1,0:T(8,128)(2,1)}, u32[]{:S(2)}, u32[]{:S(2)}) collective-permute-start(bf16[64,1,16,128]{3,2,1,0:T(8,128)(2,1)S(1)} %get-tuple-element.69), channel_id=1, source_target_pairs={{1,0},{2,1},{3,2},{4,3},{5,4},{6,5},{7,6},{0,7},{9,8},{10,9},{11,1... | collective-permute-start | bytes 786440 | tf_op jit(solution)/shard_map/ppermute | solution.py:25
  (16 other events, 30.0 us)
Sparse Core Ops, SparseCore 0:
  31.8 85.4 reduce-scatter.1
  254.2 83.9 all-reduce.10
  340.7 116.2 all-reduce.6
  460.0 118.7 all-reduce.12
  582.3 115.5 all-reduce.8
  700.1 65.3 all-gather.1
where the time goes:
time: 797 us; the launch traced here: 786 us
  waiting for transfers between devices  395 us (50%)
  local copies, waits for them, and re-layouts  150 us (19%)
  matrix products  101 us (13%)
  other arithmetic  54.6 us (7%)
  blocking collectives  34.9 us (4%)
  starting transfers between devices  34.5 us (4%)
  between operations  15.6 us (2%)
    psum x1, waiting for transfers between devices, per_device(): lax.psum(space_scatter(other_grads[0, 0]), 'dp').astype(jnp.float32)  117 us
    psum x1, waiting for transfers between devices, per_device(): enc_params = space_gather(lax.psum(enc_rows, 'dp'))  112 us
    psum x1, waiting for transfers between devices, per_device(): late_params = space_gather(lax.psum(late_rows, 'dp'))  79.7 us
    unnamed x7, waiting for transfers between devices  72.6 us
    transpose x2, matrix products, kernel_grad(): return result.transpose(2, 3, 4, 1, 0).reshape(27, channels, channels)  63.5 us
    unnamed x116, local copies, waits for them, and re-layouts  60.2 us
    all_gather x1, blocking collectives, space_gather(): whole = lax.all_gather(block, 'space', axis=0, tiled=False)  34.9 us
    conv_general_dilated x3, matrix products, forward_local(): lax.conv_general_dilated(padded[None], weights, (1, 1, 1), 'VALID', dimen...  27.5 us
  transfers between devices with their start and end apart: 18, of which 7 were waited for; matrix products, arithmetic and copies ran while one was open for 36% of the time, Pallas kernels for 0%

commit v1 on v0

--- a/solution.py
+++ b/solution.py
@@ -146,7 +146,7 @@
     enc_rows = owner_rows(
         other_tot[2:4] * scale, assignment[2:4], owner, moment_first, moment_second, master_weights
     )
-    enc_params = space_gather(lax.psum(enc_rows, "dp"))
+    enc_params = space_gather(jnp.sum(lax.all_gather(enc_rows, "dp"), axis=0))
     kernel_c = enc_params[0].reshape(27, channels, channels)
     kernel_d = enc_params[1].reshape(27, channels, channels)
     ab_grads = jnp.stack([grad_a.reshape(27, -1), grad_b.reshape(27, -1)]).astype(jnp.bfloat16)

time: 797 us -> 683 us (0.86)
  waiting for transfers between devices: 395 us -> 205 us
  blocking collectives: 34.9 us -> 109 us
    psum x1 -> x0, waiting for transfers between devices: 112 us -> none  [per_device(): enc_params = space_gather(lax.psum(enc_rows, 'dp'))]
    psum x0 -> x1, blocking collectives: none -> 53.1 us  [per_device(): ab_tot = lax.psum(space_scatter(ab_grads), 'dp').astype(jnp.float32)]
    psum x1, waiting for transfers between devices: 117 us -> 64.3 us  [per_device(): lax.psum(space_scatter(other_grads[0, 0]), 'dp').astype(jnp.float32)]
    psum x1, waiting for transfers between devices: 79.7 us -> 57 us  [per_device(): late_params = space_gather(lax.psum(late_rows, 'dp'))]
    all_gather x0 -> x1, blocking collectives: none -> 21.1 us  [per_device(): enc_params = space_gather(jnp.sum(lax.all_gather(enc_rows, 'dp'), axis=0))]
    unnamed x7 -> x6, waiting for transfers between devices: 72.6 us -> 68.1 us
    unnamed x116 -> x114, local copies, waits for them, and re-layouts: 60.2 us -> 60.9 us
  transfers between devices with their start and end apart: 18 -> 17, of which waited for: 7 -> 6; matrix products, arithmetic and copies ran while one was open for 36% -> 42% of each run, Pallas kernels for 0% -> 0%
where the time goes in v1:
time: 683 us; the launch traced here: 673 us
  waiting for transfers between devices  205 us (30%)
  local copies, waits for them, and re-layouts  154 us (23%)
  blocking collectives  109 us (16%)
  matrix products  99.9 us (15%)
  other arithmetic  55.8 us (8%)
  starting transfers between devices  34.5 us (5%)
  between operations  15.3 us (2%)
    unnamed x6, waiting for transfers between devices  68.1 us
    psum x1, waiting for transfers between devices, per_device(): lax.psum(space_scatter(other_grads[0, 0]), 'dp').astype(jnp.float32)  64.3 us
    transpose x2, matrix products, kernel_grad(): return result.transpose(2, 3, 4, 1, 0).reshape(27, channels, channels)  63.5 us
    unnamed x114, local copies, waits for them, and re-layouts  60.9 us
    psum x1, waiting for transfers between devices, per_device(): late_params = space_gather(lax.psum(late_rows, 'dp'))  57 us
    psum x1, blocking collectives, per_device(): ab_tot = lax.psum(space_scatter(ab_grads), 'dp').astype(jnp.float32)  53.1 us
    all_gather x1, blocking collectives, space_gather(): whole = lax.all_gather(block, 'space', axis=0, tiled=False)  35.1 us
    conv_general_dilated x3, matrix products, forward_local(): lax.conv_general_dilated(padded[None], weights, (1, 1, 1), 'VALID', dimen...  27.5 us
  transfers between devices with their start and end apart: 17, of which 6 were waited for; matrix products, arithmetic and copies ran while one was open for 42% of the time, Pallas kernels for 0%

profile of v1, /device:TPU:0, one launch (start us, length us, event | category | flops | bytes accessed | tf_op | source)
XLA Modules:
  0.0 672.9 jit_solution(5166762640945628211)
XLA Ops:
  9.1 3.3 collective-permute-start
  18.0 4.4 collective-permute-start.3
  22.4 3.4 reshape_squeeze.21
  25.9 2.8 copy.341
  40.1 2.6 copy.239
  48.8 5.6 collective-permute-start.7
  58.3 6.6 maximum_bitcast_fusion
  64.8 7.8 %copy.261 = bf16[64,4,18,1,130]{0,1,4,2,3:T(4,128)(2,1)S(1)} copy(bf16[64,4,18,1,130]{4,2,1,0,3:T(8,128)(2,1)} %maximum_bitcast_fusion) | data formatting | bytes 2396160
  74.9 4.6 fusion.53
  84.8 4.7 fusion.139
  89.5 5.9 copy.262
  95.4 2.9 pad.2.clone
  99.4 8.6 %fusion.50 = f32[2,16,8,17,64]{4,2,3,1,0:T(8,128)S(1)} fusion(bf16[3,3,3,64,64]{4,3,2,1,0:T(8,128)(2,1)S(1)} %copy-done.32, bf16[64,4,18,1,7,2]{0,4,5,2,1,3:T(8,128)(2,1)S(1)} %slice.228, bf16[64,4,18,1,8,17]{0,4,5,2,1,3:T(8,128)(2,1)S(1)} %copy.202, pred[8,17]{0,1:T(8,128)(4,1)S(1)} %copy-done.43), kind=kOutput, calls=%fused_computation.57 | convolution fusion | flops 967073792 | bytes 2717832 | tf_op jit(solution)/shard_map/conv_general_dilated | solution.py:38
  109.9 3.7 copy.259
  113.7 3.0 fusion.76
  119.1 5.6 collective-permute-start.11
  124.8 4.4 copy.233
  129.1 4.6 fusion.138
  133.7 12.1 %copy.232 = bf16[1,64,4,18,130]{1,0,4,3,2:T(2,128)(2,1)} copy(bf16[1,64,4,18,130]{4,1,3,2,0:T(8,128)(2,1)} %fusion.138) | data formatting | bytes 2396160 | tf_op jit(solution)/shard_map/broadcast_in_dim | solution.py:39
  150.0 2.4 fusion.114
  153.5 30.6 %convolution_convert_fusion.1 = bf16[3,3,3,64,64]{3,4,2,1,0:T(8,128)(2,1)} fusion(bf16[1,64,4,18,130]{1,0,4,3,2:T(2,128)(2,1)S(1)} %copy-done.14, bf16[64,1,2,16,128]{0,1,4,3,2:T(2,128)(2,1)S(1)} %copy-done.22), kind=kOutput, calls=%fused_computation.66 | convolution fusion | flops 906080256 | bytes 1943552 | tf_op jit(solution)/shard_map/transpose | solution.py:73
  184.2 5.2 maximum_bitcast_fusion.1
  193.4 5.7 copy.263
  199.0 2.9 pad.6.clone
  204.1 5.6 collective-permute-start.5
  213.9 9.3 %copy.238 = bf16[1,64,4,18,130]{1,0,4,3,2:T(2,128)(2,1)} copy(bf16[1,64,4,18,130]{4,1,3,2,0:T(8,128)(2,1)S(1)} %maximum_bitcast_fusion.4) | data formatting | bytes 2396160 | tf_op jit(solution)/shard_map/broadcast_in_dim | solution.py:66
  223.2 32.9 %convolution_convert_fusion = bf16[3,3,3,64,64]{3,4,2,1,0:T(8,128)(2,1)S(1)} fusion(bf16[1,64,4,18,130]{1,0,4,3,2:T(2,128)(2,1)} %copy.238, bf16[64,1,2,16,128]{0,1,4,3,2:T(2,128)(2,1)} %copy.239), kind=kOutput, calls=%fused_computation.65 | convolution fusion | flops 906080256 | bytes 1943552 | tf_op jit(solution)/shard_map/transpose | solution.py:73
  261.1 2.7 maximum_bitcast_fusion.2
  263.8 4.5 copy.264
  270.6 4.3 select_convert_fusion
  276.1 68.0 %all-reduce.9.cloned.1.call-done = bf16[8,2,27,512]{3,1,2,0:T(2,128)(2,1)} async-done(((bf16[8,2,27,512]{3,1,2,0:T(2,128)(2,1)}), bf16[8,2,27,512]{3,1,2,0:T(2,128)(2,1)}) %all-reduce.9.cloned.1.call-update) | async-done | bytes 442384
  345.5 53.1 %psum.22 = bf16[2,27,512]{2,1,0:T(8,128)(2,1)S(1)} all-reduce(bf16[2,27,512]{2,1,0:T(8,128)(2,1)S(1)} %bitcast.211), channel_id=1, replica_groups=mesh['dp'=16,'space'=8] {'dp'}, use_global_device_ids=true, to_apply=%region_4.6 | all-reduce | flops 27648 | bytes 110592 | tf_op jit(solution)/shard_map/psum | solution.py:153
  398.6 64.3 %all-reduce.5.cloned.1.call-done = bf16[12,27,512]{2,1,0:T(8,128)(2,1)} async-done(((bf16[12,27,512]{2,1,0:T(8,128)(2,1)}), bf16[12,27,512]{2,1,0:T(8,128)(2,1)}) %all-reduce.5.cloned.1.call-update) | async-done | bytes 331792 | tf_op jit(solution)/shard_map/psum | solution.py:145
  467.9 21.1 %all-gather = bf16[32,27,512]{2,1,0:T(8,128)(2,1)S(1)} all-gather(bf16[2,27,512]{2,1,0:T(8,128)(2,1)S(1)} %broadcast_select_fusion), channel_id=2, replica_groups=mesh['dp'=16,'space'=8] {'dp'}, dimensions={0}, use_global_device_ids=true | all-gather | bytes 940032 | tf_op jit(solution)/shard_map/all_gather | solution.py:149
  489.2 35.1 %all-gather.1 = bf16[16,27,512]{2,1,0:T(8,128)(2,1)S(1)} all-gather(bf16[2,27,512]{2,1,0:T(8,128)(2,1)S(1)} %reduce_sum.21), channel_id=3, replica_groups=mesh['dp'=16,'space'=8] {'space'}, dimensions={0}, use_global_device_ids=true | all-gather | bytes 497664 | tf_op jit(solution)/shard_map/all_gather | solution.py:87
  526.9 57.0 %all-reduce.7.cloned.1.call-done = bf16[1,10,27,512]{3,2,1,0:T(8,128)(2,1)} async-done(((bf16[1,10,27,512]{3,2,1,0:T(8,128)(2,1)}), bf16[1,10,27,512]{3,2,1,0:T(8,128)(2,1)}) %all-reduce.7.cloned.1.call-update) | async-done | bytes 276496 | tf_op jit(solution)/shard_map/psum | solution.py:166
  583.9 10.3 %fusion.47 = f32[2,16,8,17,64]{4,2,3,1,0:T(8,128)S(1)} fusion(bf16[3,3,3,64,64]{4,3,2,1,0:T(8,128)(2,1)S(1)} %reshape_reshape_squeeze.15, bf16[64,4,18,1,7,2]{0,4,5,2,1,3:T(8,128)(2,1)S(1)} %copy-done.35, bf16[64,4,18,1,8,17]{0,4,5,2,1,3:T(8,128)(2,1)} %copy-done.21, pred[8,17]{0,1:T(8,128)(4,1)S(1)} %copy-done.44), kind=kOutput, calls=%fused_computation.56 | convolution fusion | flops 967073792 | bytes 2717832 | tf_op jit(solution)/shard_map/conv_general_dilated | solution.py:38
  594.8 2.4 copy.260
  598.8 2.9 collective-permute-start.8
  601.7 2.8 collective-permute-start.9
  605.7 3.3 copy.251
  613.6 2.8 collective-permute-done.9
  619.1 2.7 maximum_bitcast_fusion.3
  621.8 4.9 copy.265
  628.4 8.6 %fusion.42 = f32[2,16,8,17,64]{4,2,3,1,0:T(8,128)S(1)} fusion(bf16[3,3,3,64,64]{4,3,2,1,0:T(8,128)(2,1)S(1)} %reshape_reshape_squeeze.16, bf16[64,4,18,1,7,2]{0,4,5,2,1,3:T(8,128)(2,1)S(1)} %slice.252, bf16[64,4,18,1,8,17]{0,4,5,2,1,3:T(8,128)(2,1)S(1)} %copy.228, pred[8,17]{0,1:T(8,128)(4,1)S(1)} %copy-done.44), kind=kOutput, calls=%fused_computation.55 | convolution fusion | flops 967073792 | bytes 2717832 | tf_op jit(solution)/shard_map/conv_general_dilated | solution.py:38
  640.5 11.6 %all-gather.4.cloned.1.call-done = bf16[8,10,27,512]{3,2,1,0:T(8,128)(2,1)} async-done(((bf16[1,10,27,512]{3,2,1,0:T(8,128)(2,1)}), bf16[8,10,27,512]{3,2,1,0:T(8,128)(2,1)}) %all-gather.4.cloned.1.call-update) | async-done | bytes 2211856 | tf_op jit(solution)/shard_map/all_gather | solution.py:87
  659.6 3.0 pad_maximum_fusion
  662.7 3.2 copy.253
  (228 shorter events, 98.0 us)
Async XLA Ops:
  7.2 262.9 %reduce-scatter.2.cloned.1.call-start = ((), (), s32[]{:S(2)}) async-start(), calls=%async_computation.1 | async-start | bytes 3538944 | tf_op jit(solution)/shard_map/reduce_scatter | solution.py:81
  9.1 39.7 %collective-permute-start = (bf16[64,1,16,128]{3,2,1,0:T(8,128)(2,1)}, bf16[64,1,16,128]{3,2,1,0:T(8,128)(2,1)S(1)}, u32[]{:S(2)}, u32[]{:S(2)}) collective-permute-start(bf16[64,1,16,128]{3,2,1,0:T(8,128)(2,1)} %get-tuple-element.84), channel_id=1, source_target_pairs={{0,1},{1,2},{2,3},{3,4},{4,5},{5,6},{6,7},{7,0},{8,9},{9,10},{10,1... | collective-permute-start | bytes 786440 | tf_op jit(solution)/shard_map/ppermute | solution.py:22
  12.4 42.0 %collective-permute-start.1 = (bf16[64,1,16,128]{3,2,1,0:T(8,128)(2,1)}, bf16[64,1,16,128]{3,2,1,0:T(8,128)(2,1)}, u32[]{:S(2)}, u32[]{:S(2)}) collective-permute-start(bf16[64,1,16,128]{3,2,1,0:T(8,128)(2,1)} %get-tuple-element.85), channel_id=1, source_target_pairs={{1,0},{2,1},{3,2},{4,3},{5,4},{6,5},{7,6},{0,7},{9,8},{10,9},{11,1... | collective-permute-start | bytes 786440 | tf_op jit(solution)/shard_map/ppermute | solution.py:25
  16.8 65.5 %collective-permute-start.2 = (bf16[64,1,16,128]{3,0,2,1:T(8,128)(2,1)}, bf16[64,1,16,128]{3,0,2,1:T(8,128)(2,1)}, u32[]{:S(2)}, u32[]{:S(2)}) collective-permute-start(bf16[64,1,16,128]{3,0,2,1:T(8,128)(2,1)} %get-tuple-element.82), channel_id=1, source_target_pairs={{0,1},{1,2},{2,3},{3,4},{4,5},{5,6},{6,7},{7,0},{8,9},{9,10},{10,1... | collective-permute-start | bytes 786440 | tf_op jit(solution)/shard_map/ppermute | solution.py:22
  18.0 64.3 %collective-permute-start.3 = (bf16[64,1,16,128]{3,0,2,1:T(8,128)(2,1)}, bf16[64,1,16,128]{3,0,2,1:T(8,128)(2,1)}, u32[]{:S(2)}, u32[]{:S(2)}) collective-permute-start(bf16[64,1,16,128]{3,0,2,1:T(8,128)(2,1)} %get-tuple-element.83), channel_id=1, source_target_pairs={{1,0},{2,1},{3,2},{4,3},{5,4},{6,5},{7,6},{0,7},{9,8},{10,9},{11,1... | collective-permute-start | bytes 786440 | tf_op jit(solution)/shard_map/ppermute | solution.py:25
  28.6 3.8 copy-start.41
  28.6 3.8 copy-start
  28.7 315.4 %all-reduce.9.cloned.1.call-start = ((), (), s32[]{:S(2)}) async-start(), calls=%async_computation.5 | async-start | bytes 884736
  30.5 9.6 %copy-start.1 = (bf16[1,64,2,16,128]{4,3,2,1,0:T(8,128)(2,1)S(1)}, bf16[1,64,2,16,128]{4,3,2,1,0:T(8,128)(2,1)}, u32[]{:S(2)}) copy-start(bf16[1,64,2,16,128]{4,3,2,1,0:T(8,128)(2,1)} %param.13) | copy-start | bytes 1572868
  30.5 115.3 %collective-permute-start.6 = (bf16[64,1,16,128]{3,2,1,0:T(8,128)(2,1)}, bf16[64,1,16,128]{3,2,1,0:T(8,128)(2,1)}, u32[]{:S(2)}, u32[]{:S(2)}) collective-permute-start(bf16[64,1,16,128]{3,2,1,0:T(8,128)(2,1)} %get-tuple-element.78), channel_id=1, source_target_pairs={{0,1},{1,2},{2,3},{3,4},{4,5},{5,6},{6,7},{7,0},{8,9},{9,10},{10,1... | collective-permute-start | bytes 786440 | tf_op jit(solution)/shard_map/ppermute | solution.py:22
  35.5 7.2 %copy-start.8 = (f32[2,27,512]{2,0,1:T(2,128)S(1)}, f32[2,27,512]{2,0,1:T(2,128)}, u32[]{:S(2)}) copy-start(f32[2,27,512]{2,0,1:T(2,128)} %param.20) | copy-start | bytes 331780
  37.6 6.7 copy-start.6
  40.1 5.8 copy-start.4
  40.1 7.4 %copy-start.42 = (u32[128]{0:T(128)S(1)}, u32[128]{0:T(128)}, u32[]{:S(2)}) copy-start(u32[128]{0:T(128)} %constant.154) | copy-start | bytes 1540
  48.8 97.0 %collective-permute-start.7 = (bf16[64,1,16,128]{3,2,1,0:T(8,128)(2,1)}, bf16[64,1,16,128]{3,2,1,0:T(8,128)(2,1)}, u32[]{:S(2)}, u32[]{:S(2)}) collective-permute-start(bf16[64,1,16,128]{3,2,1,0:T(8,128)(2,1)} %get-tuple-element.79), channel_id=1, source_target_pairs={{1,0},{2,1},{3,2},{4,3},{5,4},{6,5},{7,6},{0,7},{9,8},{10,9},{11,1... | collective-permute-start | bytes 786440 | tf_op jit(solution)/shard_map/ppermute | solution.py:25
  113.7 3.0 copy-start.10
  113.7 3.0 copy-start.11
  119.1 90.6 %collective-permute-start.10 = (bf16[64,1,16,128]{3,2,1,0:T(8,128)(2,1)}, bf16[64,1,16,128]{3,2,1,0:T(8,128)(2,1)}, u32[]{:S(2)}, u32[]{:S(2)}) collective-permute-start(bf16[64,1,16,128]{3,2,1,0:T(8,128)(2,1)} %get-tuple-element.74), channel_id=1, source_target_pairs={{0,1},{1,2},{2,3},{3,4},{4,5},{5,6},{6,7},{7,0},{8,9},{9,10},{10,1... | collective-permute-start | bytes 786440 | tf_op jit(solution)/shard_map/ppermute | solution.py:22
  119.1 90.6 %collective-permute-start.11 = (bf16[64,1,16,128]{3,2,1,0:T(8,128)(2,1)}, bf16[64,1,16,128]{3,2,1,0:T(8,128)(2,1)}, u32[]{:S(2)}, u32[]{:S(2)}) collective-permute-start(bf16[64,1,16,128]{3,2,1,0:T(8,128)(2,1)} %get-tuple-element.75), channel_id=1, source_target_pairs={{1,0},{2,1},{3,2},{4,3},{5,4},{6,5},{7,6},{0,7},{9,8},{10,9},{11,1... | collective-permute-start | bytes 786440 | tf_op jit(solution)/shard_map/ppermute | solution.py:25
  147.8 4.6 copy-start.22
  150.0 3.5 copy-start.14
  153.5 30.6 %copy-start.3 = (bf16[1,64,2,16,128]{4,3,2,1,0:T(8,128)(2,1)S(1)}, bf16[1,64,2,16,128]{4,3,2,1,0:T(8,128)(2,1)}, u32[]{:S(2)}) copy-start(bf16[1,64,2,16,128]{4,3,2,1,0:T(8,128)(2,1)} %param.14) | copy-start | bytes 1572868
  153.5 30.6 %copy-start.12 = (bf16[64,4,18,1]{3,2,1,0:T(8,128)(2,1)S(1)}, bf16[64,4,18,1]{3,2,1,0:T(8,128)(2,1)}, u32[]{:S(2)}) copy-start(bf16[64,4,18,1]{3,2,1,0:T(8,128)(2,1)} %get-tuple-element.48) | copy-start | bytes 27652
  153.5 30.7 %copy-start.13 = (bf16[64,4,18,1]{3,2,1,0:T(8,128)(2,1)S(1)}, bf16[64,4,18,1]{3,2,1,0:T(8,128)(2,1)}, u32[]{:S(2)}) copy-start(bf16[64,4,18,1]{3,2,1,0:T(8,128)(2,1)} %get-tuple-element.49) | copy-start | bytes 27652
  153.5 30.7 %copy-start.25 = (bf16[64,4,1,128]{3,2,1,0:T(2,128)(2,1)S(1)}, bf16[64,4,1,128]{3,2,1,0:T(2,128)(2,1)}, u32[]{:S(2)}) copy-start(bf16[64,4,1,128]{3,2,1,0:T(2,128)(2,1)} %copy-done.24) | copy-start | bytes 196612
  153.5 30.7 %copy-start.27 = (bf16[64,4,1,128]{3,2,1,0:T(2,128)(2,1)S(1)}, bf16[64,4,1,128]{3,2,1,0:T(2,128)(2,1)}, u32[]{:S(2)}) copy-start(bf16[64,4,1,128]{3,2,1,0:T(2,128)(2,1)} %copy-done.26) | copy-start | bytes 196612
  202.0 7.8 %copy-start.18 = (bf16[64,2,16,128]{3,2,1,0:T(8,128)(2,1)S(1)}, bf16[64,2,16,128]{3,2,1,0:T(8,128)(2,1)}, u32[]{:S(2)}) copy-start(bf16[64,2,16,128]{3,2,1,0:T(8,128)(2,1)} %copy-done.17) | copy-start | bytes 1572868
  202.3 8.8 %copy-start.21 = (bf16[64,4,18,1,8,17]{0,4,5,2,1,3:T(8,128)(2,1)}, bf16[64,4,18,1,8,17]{0,4,5,2,1,3:T(8,128)(2,1)S(1)}, u32[]{:S(2)}) copy-start(bf16[64,4,18,1,8,17]{0,4,5,2,1,3:T(8,128)(2,1)S(1)} %copy.215) | copy-start | bytes 3760132
  204.1 53.8 %collective-permute-start.4 = (bf16[64,1,16,128]{3,2,1,0:T(8,128)(2,1)}, bf16[64,1,16,128]{3,2,1,0:T(8,128)(2,1)}, u32[]{:S(2)}, u32[]{:S(2)}) collective-permute-start(bf16[64,1,16,128]{3,2,1,0:T(8,128)(2,1)} %get-tuple-element.80), channel_id=1, source_target_pairs={{0,1},{1,2},{2,3},{3,4},{4,5},{5,6},{6,7},{7,0},{8,9},{9,10},{10,1... | collective-permute-start | bytes 786440 | tf_op jit(solution)/shard_map/ppermute | solution.py:22
  204.1 53.8 %collective-permute-start.5 = (bf16[64,1,16,128]{3,2,1,0:T(8,128)(2,1)}, bf16[64,1,16,128]{3,2,1,0:T(8,128)(2,1)}, u32[]{:S(2)}, u32[]{:S(2)}) collective-permute-start(bf16[64,1,16,128]{3,2,1,0:T(8,128)(2,1)} %get-tuple-element.81), channel_id=1, source_target_pairs={{1,0},{2,1},{3,2},{4,3},{5,4},{6,5},{7,6},{0,7},{9,8},{10,9},{11,1... | collective-permute-start | bytes 786440 | tf_op jit(solution)/shard_map/ppermute | solution.py:25
  223.2 33.5 %copy-start.28 = (bf16[1,27,8,512]{3,2,1,0:T(8,128)(2,1)S(1)}, bf16[1,27,8,512]{3,2,1,0:T(8,128)(2,1)}, u32[]{:S(2)}) copy-start(bf16[1,27,8,512]{3,2,1,0:T(8,128)(2,1)} %stack.7) | copy-start | bytes 663556
  260.0 202.8 %all-reduce.5.cloned.1.call-start = ((), (), s32[]{:S(2)}) async-start(), calls=%async_computation.2 | async-start | bytes 786432 | tf_op jit(solution)/shard_map/psum | solution.py:145
  270.1 313.7 %all-reduce.7.cloned.1.call-start = ((), (), s32[]{:S(2)}) async-start(), calls=%async_computation.3 | async-start | bytes 655360 | tf_op jit(solution)/shard_map/psum | solution.py:166
  276.1 189.1 %copy-start.36 = (pred[2,12]{0,1:T(8,128)(4,1)S(1)}, pred[2,12]{0,1:T(8,128)(4,1)}, u32[]{:S(2)}) copy-start(pred[2,12]{0,1:T(8,128)(4,1)} %broadcast_compare_fusion) | copy-start | bytes 76
  398.6 67.3 %copy-start.5 = (f32[2,27,512]{2,0,1:T(2,128)S(1)}, f32[2,27,512]{2,0,1:T(2,128)}, u32[]{:S(2)}) copy-start(f32[2,27,512]{2,0,1:T(2,128)} %param.19) | copy-start | bytes 331780
  398.6 67.3 %copy-start.7 = (f32[2,27,512]{2,0,1:T(2,128)S(1)}, f32[2,27,512]{2,0,1:T(2,128)}, u32[]{:S(2)}) copy-start(f32[2,27,512]{2,0,1:T(2,128)} %param.18) | copy-start | bytes 331780
  398.6 67.3 %copy-start.9 = (f32[2,27,512]{2,0,1:T(2,128)S(1)}, f32[2,27,512]{2,0,1:T(2,128)}, u32[]{:S(2)}) copy-start(f32[2,27,512]{2,0,1:T(2,128)} %param.20) | copy-start | bytes 331780
  463.9 2.8 copy-start.37
  463.9 2.8 copy-start.38
  465.0 2.6 copy-start.29
  465.0 2.6 copy-start.30
  465.0 2.6 copy-start.31
  465.0 2.6 copy-start.39
  467.6 184.5 %all-gather.4.cloned.1.call-start = ((), (), s32[]{:S(2)}) async-start(), calls=%async_computation.4 | async-start | bytes 2949120 | tf_op jit(solution)/shard_map/all_gather | solution.py:87
  489.0 94.9 %copy-start.35 = (bf16[64,4,18,1,7,2]{0,4,5,2,1,3:T(8,128)(2,1)S(1)}, bf16[64,4,18,1,7,2]{0,4,5,2,1,3:T(8,128)(2,1)}, u32[]{:S(2)}) copy-start(bf16[64,4,18,1,7,2]{0,4,5,2,1,3:T(8,128)(2,1)} %slice.242) | copy-start | bytes 387076
  597.2 7.4 %copy-start.19 = (bf16[2,16,8,17,64]{4,1,3,2,0:T(8,128)(2,1)S(1)}, bf16[2,16,8,17,64]{4,1,3,2,0:T(8,128)(2,1)}, u32[]{:S(2)}) copy-start(bf16[2,16,8,17,64]{4,1,3,2,0:T(8,128)(2,1)} %copy.211) | copy-start | bytes 1671172
  598.8 14.8 %collective-permute-start.8 = (bf16[64,1,16,128]{3,2,1,0:T(8,128)(2,1)S(1)}, bf16[64,1,16,128]{3,2,1,0:T(8,128)(2,1)}, u32[]{:S(2)}, u32[]{:S(2)}) collective-permute-start(bf16[64,1,16,128]{3,2,1,0:T(8,128)(2,1)S(1)} %get-tuple-element.76), channel_id=1, source_target_pairs={{0,1},{1,2},{2,3},{3,4},{4,5},{5,6},{6,7},{7,0},{8,9},{9,10},{10,1... | collective-permute-start | bytes 786440 | tf_op jit(solution)/shard_map/ppermute | solution.py:22
  601.7 14.7 %collective-permute-start.9 = (bf16[64,1,16,128]{3,2,1,0:T(8,128)(2,1)S(1)}, bf16[64,1,16,128]{3,2,1,0:T(8,128)(2,1)}, u32[]{:S(2)}, u32[]{:S(2)}) collective-permute-start(bf16[64,1,16,128]{3,2,1,0:T(8,128)(2,1)S(1)} %get-tuple-element.77), channel_id=1, source_target_pairs={{1,0},{2,1},{3,2},{4,3},{5,4},{6,5},{7,6},{0,7},{9,8},{10,9},{11,1... | collective-permute-start | bytes 786440 | tf_op jit(solution)/shard_map/ppermute | solution.py:25
  (14 other events, 18.0 us)
Sparse Core Ops, SparseCore 0:
  28.8 86.7 reduce-scatter.1
  260.2 83.8 all-reduce.8
  346.5 116.2 all-reduce.4
  467.7 116.0 all-reduce.6
  586.0 66.0 all-gather.3
